TPU v7x, 512 devices: a whole 4x4x16 slice. The times are simulated.
512 devices in a mesh: cfg: 2 (over core), grp: 4 (over y), seq: 64 (over x, z).
Axes of the slice: x: 4, y: 4, z: 16, core: 2. Of those that a mesh axis runs over, the one named last changes fastest.
Arguments:
- query: bfloat16 [2, 4, 2, 128, 2432], P('cfg', 'grp', None, 'seq'), may hold values from -150 to 150
- keys: bfloat16 [2, 4, 2, 128, 2432], P('cfg', 'grp', None, 'seq'), may hold values from -5.5 to 5.5
- values: bfloat16 [2, 4, 2, 128, 2432], P('cfg', 'grp', None, 'seq'), may hold values from -5 to 5
- hidden: bfloat16 [2, 4, 2, 128, 2432], P('cfg', 'grp', None, 'seq'), may hold values from -23 to 23
- latent: float32 [4, 2, 128, 64], P('grp', None, 'seq', 'cfg'), may hold values from -6 to 6
- deal: int32 [4, 2], replicated, may hold values from 0 to 5, as said below
- lengths: int32 [4, 2], replicated, may hold values from 64 to 128, as said below
- w_out: bfloat16 [2432, 2432], P(('cfg', 'seq')), may hold values from -0.125 to 0.125
- attn_gate: float32 [2, 6, 2432], P('cfg'), may hold values from 0.25 to 1.75
- modulation: float32 [2, 6, 2, 2432], P('cfg'), may hold values from -3 to 3
- w_final: bfloat16 [2432, 64], replicated, may hold values from -0.125 to 0.125
- guide: float32 [6], replicated, may hold values from 2 to 7
- step_size: float32 [6], replicated, may hold values from 0.15 to 0.5
Outputs:
- latent_next: float32 [4, 2, 128, 64], P('grp', None, 'seq', 'cfg')
Inputs may be any that keep to these rules, and one draw needn't show every extreme that they name: `deal`: column 0 of row g names the whole item of group g, column 1 the item split between groups g and g xor 1 (equal in both rows); every one of the 6 items is named by exactly one column-0 entry or one pair of column-1 entries. `lengths`: in each column some group has all 128 slots live.
All inputs are finite; a program needn't handle non-finite values.
Results may differ from a plain program's by a relative error of at most 0.0049.
Values may be sent and summed in bfloat16 or wider, within the bound.
No kernel may reach another device: no remote copies, remote signals or barrier semaphores. Data moves between devices by JAX's collectives and lax.ppermute only.
A program may use at most 128 MiB of HBM per device.

v0:
```python
import jax
import jax.numpy as jnp
from jax import lax
from jax.sharding import PartitionSpec as P

D = 2432
HEADS = 38
HD = 64
NORM_EPS = 1e-06


def from_partner(x, axis, apart):
    return lax.ppermute(x, axis, [(i, i ^ 1 << apart) for i in range(lax.axis_size(axis))])


def attend(queries, keys_all, values_all, live_keys):
    row_count = queries.shape[0]
    query_heads = queries.reshape(row_count, HEADS, HD)
    key_heads = keys_all.reshape(-1, HEADS, HD)
    value_heads = values_all.reshape(-1, HEADS, HD)
    scores = jnp.einsum(
        "shd,khd->hsk", query_heads, key_heads, preferred_element_type=jnp.float32
    ) * HD ** (-0.5)
    scores = jnp.where(live_keys[None, None, :], scores, -jnp.inf)
    peak_score = jnp.max(scores, axis=2, keepdims=True)
    raw_weights = jnp.exp(scores - peak_score)
    row_total = jnp.sum(raw_weights, axis=2, keepdims=True)
    weights = raw_weights.astype(jnp.bfloat16)
    mixed_out = (
        jnp.einsum("hsk,khd->hsd", weights, value_heads, preferred_element_type=jnp.float32)
        / row_total
    )
    return jnp.transpose(mixed_out, (1, 0, 2)).reshape(row_count, HEADS * HD)


def shards(
    query,
    keys,
    values,
    hidden,
    latent,
    deal,
    lengths,
    w_out,
    attn_gate,
    modulation,
    w_final,
    guide,
    step_size,
):
    group_id = lax.axis_index("grp")
    branch = lax.axis_index("cfg")
    partner = jnp.bitwise_xor(group_id, 1)
    own_lengths = lax.dynamic_index_in_dim(lengths, group_id, 0, keepdims=False)
    pair_lengths = lax.dynamic_index_in_dim(lengths, partner, 0, keepdims=False)
    item_ids = lax.dynamic_index_in_dim(deal, group_id, 0, keepdims=False)
    resident_key_rows = keys[0, 0]
    local_values = values[0, 0]
    shard_rows = resident_key_rows.shape[1]
    far_keys, far_values = from_partner((resident_key_rows[1], local_values[1]), "grp", 0)
    combined_key_rows, joint_values = (
        lax.all_gather(
            jnp.concatenate([resident_key_rows, far_keys[None]], 0), "seq", axis=1, tiled=True
        ),
        lax.all_gather(
            jnp.concatenate([local_values, far_values[None]], 0), "seq", axis=1, tiled=True
        ),
    )
    group_keys, group_values = (combined_key_rows[:2], joint_values[:2])
    pair_keys, pair_values = (combined_key_rows[2], joint_values[2])
    slot_total = group_keys.shape[1]
    slot_ids = jnp.arange(slot_total)
    live_home = slot_ids < own_lengths[0]
    live_own = slot_ids < own_lengths[1]
    live_pair = slot_ids < pair_lengths[1]
    local_query = query[0, 0]
    local_output_rows = attend(local_query[0], group_keys[0], group_values[0], live_home)
    shared = attend(
        local_query[1],
        jnp.concatenate([group_keys[1], pair_keys], 0),
        jnp.concatenate([group_values[1], pair_values], 0),
        jnp.concatenate([live_own, live_pair], 0),
    )
    attn_rows = (
        jnp.stack([local_output_rows, shared]).astype(jnp.bfloat16).reshape(2 * shard_rows, D)
    )
    projected = jnp.dot(
        attn_rows,
        lax.all_gather(w_out, ("cfg", "seq"), axis=0, tiled=True),
        preferred_element_type=jnp.float32,
    )
    projected = projected.reshape(2, shard_rows, D)
    item_count = guide.shape[0]
    indicator_mask = (jnp.arange(item_count)[None, :] == item_ids[:, None]).astype(jnp.float32)
    gate_now = jnp.einsum(
        "ri,id->rd", indicator_mask, attn_gate[0], precision=lax.Precision.HIGHEST
    )
    stream = hidden[0, 0].astype(jnp.float32) + gate_now[:, None, :] * projected
    row_mean = jnp.mean(stream, axis=2, keepdims=True)
    centred = stream - row_mean
    row_var = jnp.mean(centred * centred, axis=2, keepdims=True)
    normed = centred * lax.rsqrt(row_var + NORM_EPS)
    selected_entries = jnp.einsum(
        "ub,bkg->ukg", indicator_mask, modulation[0], precision=lax.Precision.HIGHEST
    )
    shaped = (
        normed * (1.0 + selected_entries[:, 1][:, None, :]) + selected_entries[:, 0][:, None, :]
    ).astype(jnp.bfloat16)
    velocity = jnp.einsum("rsd,dc->rsc", shaped, w_final, preferred_element_type=jnp.float32)
    row_slots = lax.axis_index("seq") * shard_rows + jnp.arange(shard_rows)
    live_rows = jnp.stack([row_slots < own_lengths[0], row_slots < own_lengths[1]])
    velocity = jnp.where(live_rows[:, :, None], velocity, jnp.float32(0.0))
    weight_now = jnp.sum(indicator_mask * guide[None, :], axis=1)[:, None, None]
    step_now = jnp.sum(indicator_mask * step_size[None, :], axis=1)[:, None, None]
    latent_part = latent[0]
    part_width = latent_part.shape[2]
    outgoing_velocity = lax.dynamic_slice_in_dim(velocity, (1 - branch) * part_width, part_width, 2)
    own_velocity = lax.dynamic_slice_in_dim(velocity, branch * part_width, part_width, 2)
    other_velocity = from_partner(outgoing_velocity, "cfg", 0)
    is_conditional = branch == 0
    cond_velocity = jnp.where(is_conditional, own_velocity, other_velocity)
    uncond_velocity = jnp.where(is_conditional, other_velocity, own_velocity)
    guided = uncond_velocity + weight_now * (cond_velocity - uncond_velocity)
    updated = latent_part - step_now * guided
    return updated[None]


def solution(mesh):
    placed = (
        P("cfg", "grp", None, "seq", None),
        P("cfg", "grp", None, "seq", None),
        P("cfg", "grp", None, "seq", None),
        P("cfg", "grp", None, "seq", None),
        P("grp", None, "seq", "cfg"),
        P(),
        P(),
        P(("cfg", "seq"), None),
        P("cfg", None, None),
        P("cfg", None, None, None),
        P(),
        P(),
        P(),
    )
    return jax.shard_map(
        shards, mesh=mesh, in_specs=placed, out_specs=P("grp", None, "seq", "cfg"), check_vma=False
    )
```

profile of v0, /device:TPU:1, one launch (start us, length us, event | category | flops | bytes accessed | tf_op | source)
XLA Modules:
  0.0 488.3 jit_solution(13304708734672202299)
XLA Ops:
  6.5 0.0 copy-start
  6.5 0.0 all-gather.7.cloned.1.call-start
  6.5 0.8 slice_bitcast_fusion.1
  7.3 4.0 collective-permute-start.1
  11.3 0.7 copy.77
  12.1 0.3 collective-permute-done.1
  12.4 0.6 pad_maximum_fusion.1
  13.0 0.0 all-gather.7.cloned.1.call-update
  13.1 0.0 all-gather.5.cloned.1.call-start
  13.1 0.7 slice_bitcast_fusion.2
  13.8 3.4 collective-permute-start
  17.2 0.7 copy.78
  17.9 0.3 collective-permute-done
  18.2 0.6 pad_maximum_fusion
  18.9 0.0 all-gather.5.cloned.1.call-update
  18.9 0.0 all-gather.9.cloned.1.call-start
  19.0 0.7 all-gather.9.cloned.1.call-update
  19.7 0.7 fusion.67
  20.4 0.1 reshape_squeeze.15
  20.5 0.8 constant_dynamic-slice_fusion.2
  21.3 0.5 slice.67
  21.9 0.1 reshape_squeeze.13
  21.9 0.9 fusion.57
  22.8 0.6 fusion.68
  23.4 0.7 iota_compare_fusion.5
  24.1 1.3 iota_compare_fusion.3
  25.4 1.3 fusion.58
  26.8 1.0 fusion.34
  27.8 1.2 fusion.32
  29.0 122.6 %all-gather.7.cloned.1.call-done = bf16[3,128,2432]{2,0,1:T(4,128)(2,1)} async-done(((bf16[3,2,2432]{2,0,1:T(4,128)(2,1)}), bf16[3,128,2432]{2,0,1:T(4,128)(2,1)}) %all-gather.7.cloned.1.call-update) | async-done | bytes 1867792 | tf_op jit(solution)/shard_map/all_gather | solution.py:65
  151.6 7.6 %fusion.66 = (bf16[1,128,2432]{2,0,1:T(2,128)(2,1)S(1)}, bf16[1,128,2432]{2,0,1:T(2,128)(2,1)}, bf16[1,128,2432]{2,0,1:T(2,128)(2,1)S(1)}) fusion(bf16[3,128,2432]{2,0,1:T(4,128)(2,1)} %all-gather.7.cloned.1.call-done), kind=kLoop, calls=%fused_computation.84 | loop fusion | bytes 3735552 | tf_op jit(solution)/shard_map/slice | solution.py:77
  159.2 2.7 copy.57
  162.0 2.1 copy.56
  164.0 127.7 %all-gather.5.cloned.1.call-done = bf16[3,128,2432]{2,0,1:T(4,128)(2,1)} async-done(((bf16[3,2,2432]{2,0,1:T(4,128)(2,1)}), bf16[3,128,2432]{2,0,1:T(4,128)(2,1)}) %all-gather.5.cloned.1.call-update) | async-done | bytes 1867792 | tf_op jit(solution)/shard_map/all_gather | solution.py:62
  291.8 8.0 %fusion.65 = (bf16[1,128,2432]{2,0,1:T(2,128)(2,1)S(1)}, bf16[1,128,2432]{2,0,1:T(2,128)(2,1)}, bf16[1,128,2432]{2,0,1:T(2,128)(2,1)}) fusion(bf16[3,128,2432]{2,0,1:T(4,128)(2,1)} %all-gather.5.cloned.1.call-done), kind=kLoop, calls=%fused_computation.83 | loop fusion | bytes 3735552 | tf_op jit(solution)/shard_map/slice | solution.py:77
  299.8 3.6 copy.54
  303.4 3.6 copy.53
  306.9 1.7 fusion.69
  308.6 0.2 fusion.37
  308.8 0.0 copy-done.1
  308.8 0.5 fusion.28
  309.3 0.1 stack_reshape.9
  309.4 1.4 copy.51
  310.9 1.4 copy.47
  312.3 0.3 fusion.70
  312.6 0.2 fusion.41
  312.8 0.5 fusion.27
  313.3 0.1 stack_reshape.8
  313.4 0.0 copy-start.2
  313.4 141.1 %all-gather.9.cloned.1.call-done = bf16[128,19,2432]{2,1,0:T(8,128)(2,1)} async-done(((bf16[1,19,2432]{2,1,0:T(8,128)(2,1)}), bf16[128,19,2432]{2,1,0:T(8,128)(2,1)}) %all-gather.9.cloned.1.call-update) | async-done | bytes 11829264 | tf_op jit(solution)/shard_map/all_gather | solution.py:89
  454.5 16.7 %reshape.76 = bf16[2432,2432,1]{1,0,2:T(8,128)(2,1)} reshape(bf16[128,19,2432]{2,1,0:T(8,128)(2,1)} %all-gather.9.cloned.1.call-done) | data formatting | bytes 23658496
  471.2 0.0 copy-done.2
  471.2 0.0 copy-start.3
  471.3 6.2 %fusion.71 = (f32[2,2]{1,0:T(2,128)S(1)}, f32[2,2,2432]{2,1,0:T(2,128)S(1)}) fusion(bf16[2432,2432,1]{1,0,2:T(8,128)(2,1)} %reshape.76, bf16[1,2,2432]{2,1,0:T(2,128)(2,1)S(1)} %stack_reshape.9, bf16[1,2,2432]{2,1,0:T(2,128)(2,1)S(1)} %stack_reshape.8, f32[2,2432]{1,0:T(2,128)S(1)} %fusion.34, bf16[1,1,2,2,2432]{4,3,2,1,0:T(2,128)(2,1)S(1)} %copy-done.2), kind=kOutput, calls=%fused_computation.89 | convolution fusion | flops 47394812 | bytes 11926544 | tf_op jit(solution)/shard_map/dot_general | solution.py:87
  477.5 0.2 multiply_reduce_fusion
  477.7 0.0 copy-done
  477.7 0.3 convolution_select_fusion
  478.0 0.1 constant_dynamic-slice_fusion
  478.1 2.2 collective-permute-start.2
  480.2 0.0 copy-done.4
  480.2 0.0 copy-done.5
  480.2 0.2 select_reduce_fusion.1
  480.4 0.7 collective-permute-done.2
  481.1 0.7 fusion.55
  (13 shorter events, 0.1 us)
Async XLA Ops:
  6.5 471.2 %copy-start = (bf16[2432,64]{0,1:T(8,128)(2,1)S(1)}, bf16[2432,64]{0,1:T(8,128)(2,1)}, u32[]{:S(2)}) copy-start(bf16[2432,64]{0,1:T(8,128)(2,1)} %param.23) | copy-start | bytes 933892
  6.5 145.1 %all-gather.7.cloned.1.call-start = ((), (), s32[]{:S(2)}) async-start(), calls=%async_computation.1 | async-start | bytes 2529280 | tf_op jit(solution)/shard_map/all_gather | solution.py:65
  7.3 5.1 %collective-permute-start.1 = (bf16[2,2432]{1,0:T(2,128)(2,1)S(1)}, bf16[2,2432]{1,0:T(2,128)(2,1)S(1)}, u32[]{:S(2)}, u32[]{:S(2)}) collective-permute-start(bf16[2,2432]{1,0:T(2,128)(2,1)S(1)} %slice_bitcast_fusion.1), channel_id=1, source_target_pairs={{0,64},{64,0},{128,192},{192,128},{1,65},{65,1},{129,193},{193,129... | collective-permute-start | bytes 29192 | tf_op jit(solution)/shard_map/ppermute | solution.py:13
  13.1 278.7 %all-gather.5.cloned.1.call-start = ((), (), s32[]{:S(2)}) async-start(), calls=%async_computation | async-start | bytes 2529280 | tf_op jit(solution)/shard_map/all_gather | solution.py:62
  13.8 4.4 collective-permute-start
  18.9 435.6 %all-gather.9.cloned.1.call-start = ((), (), s32[]{:S(2)}) async-start(), calls=%async_computation.2 | async-start | bytes 15058944 | tf_op jit(solution)/shard_map/all_gather | solution.py:89
  306.9 1.9 copy-start.1
  313.4 157.8 %copy-start.2 = (bf16[1,1,2,2,2432]{4,3,2,1,0:T(2,128)(2,1)S(1)}, bf16[1,1,2,2,2432]{4,3,2,1,0:T(2,128)(2,1)}, u32[]{:S(2)}) copy-start(bf16[1,1,2,2,2432]{4,3,2,1,0:T(2,128)(2,1)} %param.16) | copy-start | bytes 58372
  471.2 9.0 %copy-start.4 = (f32[6]{0:T(128)S(1)}, f32[6]{0:T(128)}, u32[]{:S(2)}) copy-start(f32[6]{0:T(128)} %param.25) | copy-start | bytes 76
  471.2 9.0 %copy-start.5 = (f32[6]{0:T(128)S(1)}, f32[6]{0:T(128)}, u32[]{:S(2)}) copy-start(f32[6]{0:T(128)} %param.24) | copy-start | bytes 76
  471.2 9.9 %copy-start.3 = (f32[1,2,2,32]{3,2,1,0:T(2,128)S(1)}, f32[1,2,2,32]{3,2,1,0:T(2,128)}, u32[]{:S(2)}) copy-start(f32[1,2,2,32]{3,2,1,0:T(2,128)} %param.17) | copy-start | bytes 1540
  478.1 3.1 collective-permute-start.2
Sparse Core Ops, SparseCore 0:
  13.2 138.4 all-gather.6
  154.6 137.1 all-gather.4
  294.8 159.6 all-gather.8
where the time goes:
time: 490 us; the launch traced here: 488 us
  waiting for transfers between devices  393 us (80%)
  local copies, waits for them, and re-layouts  54.1 us (11%)
  between operations  13.3 us (3%)
  matrix products  11.7 us (2%)
  starting transfers between devices  9.63 us (2%)
  other arithmetic  6.06 us (1%)
    all_gather x1, waiting for transfers between devices, shards(): lax.all_gather(w_out, ('cfg', 'seq'), axis=0, tiled=True)  141 us
    all_gather x1, waiting for transfers between devices, shards(): lax.all_gather(jnp.concatenate([resident_key_rows, far_keys[None]], 0), '...  128 us
    all_gather x1, waiting for transfers between devices, shards(): lax.all_gather(jnp.concatenate([local_values, far_values[None]], 0), 'seq...  123 us
    unnamed x15, local copies, waits for them, and re-layouts  18.2 us
  transfers between devices with their start and end apart: 6, of which 6 were waited for; matrix products, arithmetic and copies ran while one was open for 9% of the time, Pallas kernels for 0%

commit v1 on v0

--- a/solution.py
+++ b/solution.py
@@ -1,3 +1,4 @@
+import functools
 import jax
 import jax.numpy as jnp
 from jax import lax
@@ -7,6 +8,17 @@
 HEADS = 38
 HD = 64
 NORM_EPS = 1e-06
+
+
+def manage_joints_by_axis(vec, across):
+    shares = lax.axis_size(across)
+    slots = []
+    for dev in range(vec.ndim):
+        slots.append(shares if dev == 1 else 1)
+    return lax.all_to_all(jnp.tile(vec, slots), across, split_axis=1, concat_axis=1, tiled=True)
+
+
+draw_lane_now = functools.partial(manage_joints_by_axis, across="seq")
 
 
 def from_partner(x, axis, apart):
@@ -59,9 +71,7 @@
     shard_rows = resident_key_rows.shape[1]
     far_keys, far_values = from_partner((resident_key_rows[1], local_values[1]), "grp", 0)
     combined_key_rows, joint_values = (
-        lax.all_gather(
-            jnp.concatenate([resident_key_rows, far_keys[None]], 0), "seq", axis=1, tiled=True
-        ),
+        draw_lane_now(jnp.concatenate([resident_key_rows, far_keys[None]], 0)),
         lax.all_gather(
             jnp.concatenate([local_values, far_values[None]], 0), "seq", axis=1, tiled=True
         ),

time: 490 us -> 375 us (0.77)
  waiting for transfers between devices: 393 us -> 263 us
  starting transfers between devices: 9.63 us -> 27.8 us
    all_gather x1 -> x0, waiting for transfers between devices: 128 us -> none  [shards(): lax.all_gather(jnp.concatenate([resident_key_rows, far_keys[None]], 0), '...]
    all_to_all x0 -> x1, starting transfers between devices: none -> 18.2 us  [manage_joints_by_axis(): lax.all_to_all(jnp.tile(vec, slots), across, split_axis=1, concat_axis=1,...]
    all_gather x1, waiting for transfers between devices: 141 us -> 127 us  [shards(): lax.all_gather(w_out, ('cfg', 'seq'), axis=0, tiled=True)]
    all_gather x1, waiting for transfers between devices: 123 us -> 133 us  [shards(): lax.all_gather(jnp.concatenate([local_values, far_values[None]], 0), 'seq...]
    unnamed x15 -> x31, local copies, waits for them, and re-layouts: 18.2 us -> 18.3 us
  transfers between devices with their start and end apart: 6 -> 6, of which waited for: 6 -> 5; matrix products, arithmetic and copies ran while one was open for 9% -> 11% of each run, Pallas kernels for 0% -> 0%
where the time goes in v1:
time: 375 us; the launch traced here: 374 us
  waiting for transfers between devices  263 us (70%)
  local copies, waits for them, and re-layouts  52.6 us (14%)
  starting transfers between devices  27.8 us (7%)
  between operations  13.7 us (4%)
  matrix products  10.1 us (3%)
  other arithmetic  6.07 us (2%)
    all_gather x1, waiting for transfers between devices, shards(): lax.all_gather(jnp.concatenate([local_values, far_values[None]], 0), 'seq...  133 us
    all_gather x1, waiting for transfers between devices, shards(): lax.all_gather(w_out, ('cfg', 'seq'), axis=0, tiled=True)  127 us
    unnamed x31, local copies, waits for them, and re-layouts  18.3 us
    all_to_all x1, starting transfers between devices, manage_joints_by_axis(): lax.all_to_all(jnp.tile(vec, slots), across, split_axis=1, concat_axis=1,...  18.2 us
    slice x2, local copies, waits for them, and re-layouts, shards(): group_values[0]  10.7 us
    ppermute x3, starting transfers between devices, from_partner(): lax.ppermute(x, axis, [(i, i ^ 1 << apart) for i in range(lax.axis_size(a...  9.55 us
  transfers between devices with their start and end apart: 6, of which 5 were waited for; matrix products, arithmetic and copies ran while one was open for 11% of the time, Pallas kernels for 0%

profile of v1, /device:TPU:1, one launch (start us, length us, event | category | flops | bytes accessed | tf_op | source)
XLA Modules:
  0.0 373.6 jit_solution(11829988478759540813)
XLA Ops:
  6.5 0.0 copy-start
  6.5 0.0 all-gather.4.cloned.1.call-start
  6.5 0.8 slice_bitcast_fusion.1
  7.3 4.0 %collective-permute-start.1 = (bf16[2,2432]{1,0:T(2,128)(2,1)S(1)}, bf16[2,2432]{1,0:T(2,128)(2,1)S(1)}, u32[]{:S(2)}, u32[]{:S(2)}) collective-permute-start(bf16[2,2432]{1,0:T(2,128)(2,1)S(1)} %slice_bitcast_fusion.1), channel_id=1, source_target_pairs={{0,64},{64,0},{128,192},{192,128},{1,65},{65,1},{129,193},{193,129... | collective-permute-start | bytes 29192 | tf_op jit(solution)/shard_map/ppermute | solution.py:25
  11.3 0.7 copy.75
  12.1 0.3 collective-permute-done.1
  12.4 0.7 pad_maximum_fusion
  13.0 0.0 all-gather.4.cloned.1.call-update
  13.1 0.0 all-gather.6.cloned.1.call-start
  13.1 0.7 all-gather.6.cloned.1.call-update
  13.8 0.7 slice_bitcast_fusion.2
  14.5 3.4 collective-permute-start
  17.9 1.4 collective-permute-done
  19.3 0.8 pad_maximum_fusion.1
  20.1 2.1 tile.4.clone
  22.1 0.0 copy-start.5
  22.2 18.2 %all-to-all-start = ((bf16[3,128,2432]{2,0,1:T(4,128)(2,1)}), bf16[3,128,2432]{2,0,1:T(4,128)(2,1)S(1)}, u32[]{:S(2)}, u32[]{:S(2)}) async-start(bf16[3,128,2432]{2,0,1:T(4,128)(2,1)} %bitcast.65), calls=%async_computation | async-start | bytes 4980736 | tf_op jit(solution)/shard_map/all_to_all | solution.py:18
  40.4 0.0 copy-done.8
  40.5 0.1 reshape_squeeze.15
  40.6 0.0 copy-done.9
  40.6 0.1 constant_dynamic-slice_fusion.2
  40.6 0.5 slice.67
  41.2 0.1 reshape_squeeze.13
  41.3 0.0 copy-done.11
  41.3 0.2 fusion.57
  41.5 0.6 fusion.68
  42.0 0.6 iota_compare_fusion.5
  42.7 1.3 iota_compare_fusion.3
  44.0 1.3 fusion.58
  45.3 0.0 copy-done.6
  45.3 0.2 fusion.34
  45.5 0.0 copy-done.5
  45.5 0.3 fusion.32
  45.8 133.1 %all-gather.4.cloned.1.call-done = bf16[3,128,2432]{2,0,1:T(4,128)(2,1)} async-done(((bf16[3,2,2432]{2,0,1:T(4,128)(2,1)}), bf16[3,128,2432]{2,0,1:T(4,128)(2,1)}) %all-gather.4.cloned.1.call-update) | async-done | bytes 1867792 | tf_op jit(solution)/shard_map/all_gather | solution.py:75
  178.9 8.0 %fusion.66 = (bf16[1,128,2432]{2,0,1:T(2,128)(2,1)}, bf16[1,128,2432]{2,0,1:T(2,128)(2,1)}, bf16[1,128,2432]{2,0,1:T(2,128)(2,1)}) fusion(bf16[3,128,2432]{2,0,1:T(4,128)(2,1)} %all-gather.4.cloned.1.call-done), kind=kLoop, calls=%fused_computation.83 | loop fusion | bytes 3735552 | tf_op jit(solution)/shard_map/slice | solution.py:87
  186.9 3.6 copy.54
  190.4 3.6 copy.53
  194.1 2.7 copy.48
  196.8 0.0 all-to-all-done
  196.8 3.8 %fusion.65 = (bf16[1,128,2432]{2,0,1:T(2,128)(2,1)}, bf16[1,128,2432]{2,0,1:T(2,128)(2,1)}, bf16[1,128,2432]{2,0,1:T(2,128)(2,1)}) fusion(bf16[3,128,2432]{2,0,1:T(4,128)(2,1)S(1)} %all-to-all-done), kind=kLoop, calls=%fused_computation.82 | loop fusion | bytes 3735552 | tf_op jit(solution)/shard_map/slice | solution.py:87
  200.7 3.7 copy.51
  204.4 2.0 copy.50
  206.4 1.7 fusion.69
  208.2 0.2 fusion.37
  208.4 0.5 fusion.28
  208.9 0.1 stack_reshape.9
  209.0 0.7 copy-done.1
  209.7 1.4 copy.44
  211.1 0.4 fusion.70
  211.4 0.2 fusion.41
  211.6 0.5 fusion.27
  212.1 0.1 stack_reshape.8
  212.2 0.0 copy-start.7
  212.2 127.2 %all-gather.6.cloned.1.call-done = bf16[128,19,2432]{2,1,0:T(8,128)(2,1)} async-done(((bf16[1,19,2432]{2,1,0:T(8,128)(2,1)}), bf16[128,19,2432]{2,1,0:T(8,128)(2,1)}) %all-gather.6.cloned.1.call-update) | async-done | bytes 11829264 | tf_op jit(solution)/shard_map/all_gather | solution.py:99
  339.4 16.8 %reshape.80 = bf16[2432,2432,1]{1,0,2:T(8,128)(2,1)} reshape(bf16[128,19,2432]{2,1,0:T(8,128)(2,1)} %all-gather.6.cloned.1.call-done) | data formatting | bytes 23658496
  356.2 0.0 copy-start.10
  356.2 6.2 %fusion.71 = (f32[2,2]{1,0:T(2,128)S(1)}, f32[2,2,2432]{2,1,0:T(2,128)S(1)}) fusion(bf16[2432,2432,1]{1,0,2:T(8,128)(2,1)} %reshape.80, bf16[1,2,2432]{2,1,0:T(2,128)(2,1)S(1)} %stack_reshape.9, bf16[1,2,2432]{2,1,0:T(2,128)(2,1)S(1)} %stack_reshape.8, f32[2,2432]{1,0:T(2,128)S(1)} %fusion.34, bf16[1,1,2,2,2432]{4,3,2,1,0:T(2,128)(2,1)S(1)} %copy-done.7), kind=kOutput, calls=%fused_computation.88 | convolution fusion | flops 47394812 | bytes 11926544 | tf_op jit(solution)/shard_map/dot_general | solution.py:97
  362.5 0.2 multiply_reduce_fusion
  362.7 0.3 convolution_select_fusion
  362.9 0.1 constant_dynamic-slice_fusion
  363.0 2.2 collective-permute-start.2
  365.2 0.2 select_reduce_fusion.1
  365.4 0.7 collective-permute-done.2
  366.1 0.7 fusion.55
  (28 shorter events, 0.1 us)
Async XLA Ops:
  6.5 356.1 %copy-start = (bf16[2432,64]{0,1:T(8,128)(2,1)S(1)}, bf16[2432,64]{0,1:T(8,128)(2,1)}, u32[]{:S(2)}) copy-start(bf16[2432,64]{0,1:T(8,128)(2,1)} %param.23) | copy-start | bytes 933892
  6.5 172.3 %all-gather.4.cloned.1.call-start = ((), (), s32[]{:S(2)}) async-start(), calls=%async_computation.1 | async-start | bytes 2529280 | tf_op jit(solution)/shard_map/all_gather | solution.py:75
  7.3 5.1 %collective-permute-start.1 = (bf16[2,2432]{1,0:T(2,128)(2,1)S(1)}, bf16[2,2432]{1,0:T(2,128)(2,1)S(1)}, u32[]{:S(2)}, u32[]{:S(2)}) collective-permute-start(bf16[2,2432]{1,0:T(2,128)(2,1)S(1)} %slice_bitcast_fusion.1), channel_id=1, source_target_pairs={{0,64},{64,0},{128,192},{192,128},{1,65},{65,1},{129,193},{193,129... | collective-permute-start | bytes 29192 | tf_op jit(solution)/shard_map/ppermute | solution.py:25
  13.1 326.4 %all-gather.6.cloned.1.call-start = ((), (), s32[]{:S(2)}) async-start(), calls=%async_computation.2 | async-start | bytes 15058944 | tf_op jit(solution)/shard_map/all_gather | solution.py:99
  14.5 4.7 %collective-permute-start = (bf16[2,2432]{1,0:T(2,128)(2,1)S(1)}, bf16[2,2432]{1,0:T(2,128)(2,1)S(1)}, u32[]{:S(2)}, u32[]{:S(2)}) collective-permute-start(bf16[2,2432]{1,0:T(2,128)(2,1)S(1)} %slice_bitcast_fusion.2), channel_id=1, source_target_pairs={{0,64},{64,0},{128,192},{192,128},{1,65},{65,1},{129,193},{193,129... | collective-permute-start | bytes 29192 | tf_op jit(solution)/shard_map/ppermute | solution.py:25
  22.1 18.3 %copy-start.8 = (bf16[1,1,2,2,2432]{4,3,2,1,0:T(2,128)(2,1)S(1)}, bf16[1,1,2,2,2432]{4,3,2,1,0:T(2,128)(2,1)}, u32[]{:S(2)}) copy-start(bf16[1,1,2,2,2432]{4,3,2,1,0:T(2,128)(2,1)} %param.13) | copy-start | bytes 58372
  22.1 18.4 %copy-start.9 = (s32[4,2]{0,1:T(2,128)S(1)}, s32[4,2]{0,1:T(2,128)}, u32[]{:S(2)}) copy-start(s32[4,2]{0,1:T(2,128)} %param.19) | copy-start | bytes 100
  22.1 19.1 %copy-start.11 = (s32[4,2]{0,1:T(2,128)S(1)}, s32[4,2]{0,1:T(2,128)}, u32[]{:S(2)}) copy-start(s32[4,2]{0,1:T(2,128)} %param.18) | copy-start | bytes 100
  22.1 23.1 %copy-start.6 = (f32[1,6,2432]{2,0,1:T(1,128)S(1)}, f32[1,6,2432]{2,0,1:T(1,128)}, u32[]{:S(2)}) copy-start(f32[1,6,2432]{2,0,1:T(1,128)} %param.21) | copy-start | bytes 175108
  22.1 23.4 %copy-start.5 = (f32[1,6,2,2432]{3,2,1,0:T(2,128)S(1)}, f32[1,6,2,2432]{3,2,1,0:T(2,128)}, u32[]{:S(2)}) copy-start(f32[1,6,2,2432]{3,2,1,0:T(2,128)} %param.22) | copy-start | bytes 350212
  22.2 174.6 %all-to-all-start = ((bf16[3,128,2432]{2,0,1:T(4,128)(2,1)}), bf16[3,128,2432]{2,0,1:T(4,128)(2,1)S(1)}, u32[]{:S(2)}, u32[]{:S(2)}) async-start(bf16[3,128,2432]{2,0,1:T(4,128)(2,1)} %bitcast.65), calls=%async_computation | async-start | bytes 4980736 | tf_op jit(solution)/shard_map/all_to_all | solution.py:18
  200.7 3.7 copy-start.2
  206.4 1.9 copy-start.3
  206.4 1.9 copy-start.4
  208.4 1.3 copy-start.1
  212.2 144.0 %copy-start.7 = (bf16[1,1,2,2,2432]{4,3,2,1,0:T(2,128)(2,1)S(1)}, bf16[1,1,2,2,2432]{4,3,2,1,0:T(2,128)(2,1)}, u32[]{:S(2)}) copy-start(bf16[1,1,2,2,2432]{4,3,2,1,0:T(2,128)(2,1)} %param.16) | copy-start | bytes 58372
  356.2 9.0 %copy-start.12 = (f32[6]{0:T(128)S(1)}, f32[6]{0:T(128)}, u32[]{:S(2)}) copy-start(f32[6]{0:T(128)} %param.25) | copy-start | bytes 76
  356.2 9.0 %copy-start.13 = (f32[6]{0:T(128)S(1)}, f32[6]{0:T(128)}, u32[]{:S(2)}) copy-start(f32[6]{0:T(128)} %param.24) | copy-start | bytes 76
  356.2 9.9 %copy-start.10 = (f32[1,2,2,32]{3,2,1,0:T(2,128)S(1)}, f32[1,2,2,32]{3,2,1,0:T(2,128)}, u32[]{:S(2)}) copy-start(f32[1,2,2,32]{3,2,1,0:T(2,128)} %param.17) | copy-start | bytes 1540
  363.0 3.1 collective-permute-start.2
Sparse Core Ops, SparseCore 0:
  13.2 165.6 all-gather.3
  181.9 157.4 all-gather.5
